TPU v7x, 256 devices: a whole 4x4x8 slice. The times are simulated.
256 devices in a mesh: space: 32 (over z, x), mode: 8 (over y, core).
Axes of the slice: x: 4, y: 4, z: 8, core: 2. Of those that a mesh axis runs over, the one named last changes fastest.
Arguments:
- vectors: float32 [55296, 256], P('space', 'mode'), may hold values from -6 to 6
- force_blocks: float32 [288, 27, 192, 192], P('space', None, 'mode'), as said below
- inverse_blocks: float32 [288, 192, 192], P('space'), as said below
- neighbours: int32 [288, 27], P('space'), may hold values from 0 to 287, as said below
Outputs:
- w_block: float32 [55296, 256], P('space', 'mode')
- hw_block: float32 [55296, 256], P('space', 'mode')
- gram_a: float32 [512, 2, 256], P(None, None, 'mode')
- gram_b: float32 [512, 2, 256], P(None, None, 'mode')
Inputs may be any that keep to these rules, and one draw needn't show every extreme that they name: `neighbours`: block rows are atom cells on a periodic grid of 32 layers of 3 x 3 cells; the rows of layer z are z * 9 to z * 9 + 8 in some order. Entry k = 9 (dz + 1) + 3 (dy + 1) + (dx + 1) of row i is the block row of the cell at offset (dz, dy, dx) from row i's cell, so entry 13 is i itself. H is symmetric: force_blocks[neighbours[i, k], 26 - k] is the transpose of force_blocks[i, k]. `inverse_blocks`: every block is symmetric.
All inputs are finite; a program needn't handle non-finite values.
Results may differ from a plain program's by a relative error of at most 0.00013.
Values sent between devices are 32-bit elements; how exact they have to be, the bound alone decides.
No kernel may reach another device: no remote copies, remote signals or barrier semaphores. Data moves between devices by JAX's collectives and lax.ppermute only.
A program may use at most 128 MiB of HBM per device.

v0:
```python
import jax
import jax.numpy as jnp
from jax import lax
from jax.sharding import PartitionSpec as P

CELLS = 9


def extended_2(block, sides, width):
    for axis, dim in sides:
        count = lax.axis_size(axis)
        forward = [(i, i + 1) for i in range(count - 1)]
        forward.append((count - 1, 0))
        backward = [(target, source) for source, target in forward]
        low = lax.ppermute(
            lax.slice_in_dim(block, block.shape[dim] - width, None, axis=dim), axis, forward
        )
        high = lax.ppermute(lax.slice_in_dim(block, 0, width, axis=dim), axis, backward)
        block = jnp.concatenate([low, block, high], axis=dim)
    return block


def apply_local(force_blocks, local_ids, extended):

    def accumulate(totals, offset):
        gathered = jnp.take(extended, local_ids[:, offset], axis=0)
        force_slice = lax.dynamic_index_in_dim(force_blocks, offset, 1, keepdims=False)
        product = jnp.einsum(
            "brc,bcm->brm",
            force_slice,
            gathered,
            precision=lax.Precision.HIGHEST,
            preferred_element_type=jnp.float32,
        )
        return (totals + product, None)

    initial = jnp.zeros(
        (force_blocks.shape[0], force_blocks.shape[2], extended.shape[2]), jnp.float32
    )
    totals, unused = lax.scan(
        accumulate, initial, jnp.arange(force_blocks.shape[1], dtype=jnp.int32)
    )
    regrouped = lax.all_to_all(totals, "mode", split_axis=2, concat_axis=1, tiled=True)
    return regrouped.reshape(-1, regrouped.shape[2])


def spread_search(search_field):
    gathered = lax.all_gather(search_field, "mode", axis=2, tiled=True)
    extended = extended_2(gathered, (("space", 0),), CELLS)
    return (gathered, extended)


def local_gram(flat_x, full_w, vectors, w_local, image_x, image_w, total_rows):
    basis = jnp.concatenate([flat_x, full_w.reshape(flat_x.shape)], axis=1)
    columns = jnp.stack([vectors, w_local, image_x, image_w], axis=1)
    return (
        jnp.einsum(
            "ra,rgj->agj",
            basis,
            columns,
            precision=lax.Precision.HIGHEST,
            preferred_element_type=jnp.float32,
        )
        / total_rows
    )


def local(vectors, force_blocks, inverse_blocks, neighbours):
    row_count, col_count = vectors.shape
    block_size = inverse_blocks.shape[1]
    block_rows = row_count // block_size
    slab_count = lax.axis_size("space")
    total_rows = row_count * slab_count
    own_layers = block_rows // CELLS
    layer_total = own_layers * slab_count
    slab_index = lax.axis_index("space")
    layer_of = neighbours // CELLS
    relative = (layer_of - slab_index * own_layers + 1) % layer_total
    local_ids = relative * CELLS + neighbours % CELLS
    stacked_x = vectors.reshape(block_rows, block_size, col_count)
    full_x = lax.all_gather(stacked_x, "mode", axis=2, tiled=True)
    extended_x = extended_2(full_x, (("space", 0),), CELLS)
    mode_count = full_x.shape[2]
    image_x = apply_local(force_blocks, local_ids, extended_x)
    flat_x = full_x.reshape(row_count, mode_count)
    rayleigh = lax.psum(
        jnp.einsum(
            "ra,rj->aj",
            flat_x,
            image_x,
            precision=lax.Precision.HIGHEST,
            preferred_element_type=jnp.float32,
        )
        / total_rows,
        "space",
    )
    residual = image_x - jnp.dot(
        flat_x, rayleigh, precision=lax.Precision.HIGHEST, preferred_element_type=jnp.float32
    )
    search_raw = jnp.einsum(
        "brc,bcm->brm",
        inverse_blocks,
        residual.reshape(block_rows, block_size, col_count),
        precision=lax.Precision.HIGHEST,
        preferred_element_type=jnp.float32,
    )
    squares = lax.psum(jnp.sum(search_raw * search_raw, axis=(0, 1)), "space")
    scales = lax.rsqrt(squares / total_rows + 1e-06)
    search_field = search_raw * scales
    full_w, extended_w = spread_search(search_field)
    hw_block = apply_local(force_blocks, local_ids, extended_w)
    w_block = search_field.reshape(row_count, col_count)
    gram_sum = lax.psum(
        local_gram(flat_x, full_w, vectors, w_block, image_x, hw_block, total_rows), "space"
    )
    gram_b = gram_sum[:, 0:2]
    gram_a = gram_sum[:, 2:4]
    return (w_block, hw_block, gram_a, gram_b)


def solution(mesh):
    in_specs = (
        P("space", "mode"),
        P("space", None, "mode", None),
        P("space", None, None),
        P("space", None),
    )
    out_specs = (
        P("space", "mode"),
        P("space", "mode"),
        P(None, None, "mode"),
        P(None, None, "mode"),
    )
    return jax.shard_map(local, mesh=mesh, in_specs=in_specs, out_specs=out_specs, check_vma=False)
```

profile of v0, /device:TPU:8, one launch (start us, length us, event | category | flops | bytes accessed | tf_op | source)
XLA Modules:
  0.0 1128.0 jit_solution(3499977427174082303)
XLA Ops:
  9.4 30.6 %all-gather.3.cloned.1.call-done = f32[9,192,256]{1,2,0:T(8,128)} async-done(((f32[9,192,32]{1,2,0:T(8,128)}), f32[9,192,256]{1,2,0:T(8,128)}) %all-gather.3.cloned.1.call-update) | async-done | bytes 1769488 | tf_op jit(solution)/shard_map/all_gather | solution.py:81
  42.0 5.5 collective-permute-start.1
  48.3 5.7 copy.80
  54.6 31.2 %collective-permute-done.1 = f32[9,192,256]{2,1,0:T(8,128)} collective-permute-done((f32[9,192,256]{2,1,0:T(8,128)S(1)}, f32[9,192,256]{2,1,0:T(8,128)}, u32[]{:S(2)}, u32[]{:S(2)}) %collective-permute-start.1) | collective-permute-done | bytes 1769504 | tf_op jit(solution)/shard_map/ppermute | solution.py:18
  94.4 5.2 pad_maximum_fusion
  99.6 7.6 copy.81
  107.2 248.9 %while.22 = (s32[]{:T(128)}, f32[9,24,256]{2,1,0:T(8,128)}, s32[27]{0:T(128)S(1)}, f32[9,27,24,192]{3,2,0,1:T(8,128)}, s32[9,27]{0,1:T(8,128)}, /*index=5*/f32[2...) while((s32[]{:T(128)}, f32[9,24,256]{2,1,0:T(8,128)}, s32[27]{0:T(128)S(1)}, ...), condition=%wide.region_1.3_spmd.clone, body=%wide.region_0.2_spmd.clone.sunk | while | flops 127956024 | bytes 5976391 | solution.py:40
  110.4 3.2 gather_fusion
  128.8 3.2 gather_fusion
  156.4 3.2 gather_fusion
  230.2 3.2 gather_fusion
  304.0 3.2 gather_fusion
  331.6 3.2 gather_fusion
  356.1 3.4 copy.82
  361.9 10.4 all_to_all.30
  375.9 3.5 copy.104
  384.2 141.0 %psum.21 = f32[256,32]{0,1:T(8,128)} all-reduce(f32[256,32]{0,1:T(8,128)} %fusion.27), channel_id=1, replica_groups=mesh['space'=32,'mode'=8] {'space'}, use_global_device_ids=true, to_apply=%region_2.4 | all-reduce | flops 8192 | bytes 65536 | tf_op jit(solution)/shard_map/psum | solution.py:86
  525.2 3.3 fusion.26
  530.4 3.6 multiply_reduce_fusion
  533.9 69.6 %psum.22 = f32[32]{0:T(128)S(1)} all-reduce(f32[32]{0:T(128)S(1)} %get-tuple-element.203), channel_id=1, replica_groups=mesh['space'=32,'mode'=8] {'space'}, use_global_device_ids=true, to_apply=%region_4.6 | all-reduce | flops 32 | bytes 256 | tf_op jit(solution)/shard_map/psum | solution.py:107
  605.4 25.1 %all-gather.5.cloned.1.call-done = f32[9,192,256]{1,2,0:T(8,128)} async-done(((f32[9,192,32]{1,2,0:T(8,128)}), f32[9,192,256]{1,2,0:T(8,128)}) %all-gather.5.cloned.1.call-update) | async-done | bytes 1769488 | tf_op jit(solution)/shard_map/all_gather | solution.py:48
  632.5 5.5 collective-permute-start.3
  638.1 38.3 %collective-permute-done.3 = f32[9,192,256]{2,1,0:T(8,128)} collective-permute-done((f32[9,192,256]{2,1,0:T(8,128)S(1)}, f32[9,192,256]{2,1,0:T(8,128)}, u32[]{:S(2)}, u32[]{:S(2)}) %collective-permute-start.3) | collective-permute-done | bytes 1769504 | tf_op jit(solution)/shard_map/ppermute | solution.py:18
  684.9 5.2 pad_maximum_fusion.1
  690.2 7.6 copy.92
  697.8 248.9 %while.23 = (s32[]{:T(128)}, f32[9,24,256]{2,1,0:T(8,128)}, s32[27]{0:T(128)S(1)}, f32[9,27,24,192]{3,2,0,1:T(8,128)}, s32[9,27]{0,1:T(8,128)}, /*index=5*/f32[2...) while((s32[]{:T(128)}, f32[9,24,256]{2,1,0:T(8,128)}, s32[27]{0:T(128)S(1)}, ...), condition=%wide.region_6.8_spmd.clone, body=%wide.region_5.7_spmd.clone.sunk | while | flops 127956024 | bytes 5976391 | solution.py:40
  756.2 3.2 gather_fusion.1
  830.0 3.2 gather_fusion.1
  946.6 3.5 copy.93
  953.3 5.4 all-to-all-start.1
  960.0 4.4 all-to-all-done.1
  980.4 139.4 %all-reduce.2.cloned.1.call-done = f32[512,4,32]{0,2,1:T(8,128)} async-done(((f32[512,4,32]{0,2,1:T(8,128)}), f32[512,4,32]{0,2,1:T(8,128)}) %all-reduce.2.cloned.1.call-update) | async-done | bytes 262160 | tf_op jit(solution)/shard_map/psum | solution.py:113
  (333 shorter events, 428.2 us)
Async XLA Ops:
  7.2 523.2 %copy-start = (f32[9,192,192]{2,1,0:T(8,128)S(1)}, f32[9,192,192]{2,1,0:T(8,128)}, u32[]{:S(2)}) copy-start(f32[9,192,192]{2,1,0:T(8,128)} %param.12) | copy-start | bytes 3981316
  7.2 32.8 %all-gather.3.cloned.1.call-start = ((), (), s32[]{:S(2)}) async-start(), calls=%async_computation.2 | async-start | bytes 2654208 | tf_op jit(solution)/shard_map/all_gather | solution.py:81
  9.3 621.2 %all-gather.5.cloned.1.call-start = ((), (), s32[]{:S(2)}) async-start(), calls=%async_computation.3 | async-start | bytes 2654208 | tf_op jit(solution)/shard_map/all_gather | solution.py:48
  42.0 12.0 %copy-start.2 = (f32[9,192,256]{2,1,0:T(8,128)}, f32[9,192,256]{2,1,0:T(8,128)S(1)}, u32[]{:S(2)}) copy-start(f32[9,192,256]{2,1,0:T(8,128)S(1)} %copy.76) | copy-start | bytes 5308420
  42.0 43.8 %collective-permute-start.1 = (f32[9,192,256]{2,1,0:T(8,128)S(1)}, f32[9,192,256]{2,1,0:T(8,128)}, u32[]{:S(2)}, u32[]{:S(2)}) collective-permute-start(f32[9,192,256]{2,1,0:T(8,128)S(1)} %copy.76), channel_id=1, source_target_pairs={{8,0},{16,8},{24,16},{32,24},{40,32},{48,40},{56,48},{64,56},{72,6... | collective-permute-start | bytes 5308424 | tf_op jit(solution)/shard_map/ppermute | solution.py:18
  47.5 43.9 %collective-permute-start = (f32[9,192,256]{2,1,0:T(8,128)S(1)}, f32[9,192,256]{2,1,0:T(8,128)}, u32[]{:S(2)}, u32[]{:S(2)}) collective-permute-start(f32[9,192,256]{2,1,0:T(8,128)S(1)} %copy.76), channel_id=1, source_target_pairs={{0,8},{8,16},{16,24},{24,32},{32,40},{40,48},{48,56},{56,64},{64,7... | collective-permute-start | bytes 5308424 | tf_op jit(solution)/shard_map/ppermute | solution.py:15
  375.9 5.8 copy-start.3
  632.5 52.4 %copy-start.7 = (f32[9,192,256]{2,1,0:T(8,128)}, f32[9,192,256]{2,1,0:T(8,128)S(1)}, u32[]{:S(2)}) copy-start(f32[9,192,256]{2,1,0:T(8,128)S(1)} %copy.87) | copy-start | bytes 5308420
  632.5 43.8 %collective-permute-start.3 = (f32[9,192,256]{2,1,0:T(8,128)S(1)}, f32[9,192,256]{2,1,0:T(8,128)}, u32[]{:S(2)}, u32[]{:S(2)}) collective-permute-start(f32[9,192,256]{2,1,0:T(8,128)S(1)} %copy.87), channel_id=1, source_target_pairs={{8,0},{16,8},{24,16},{32,24},{40,32},{48,40},{56,48},{64,56},{72,6... | collective-permute-start | bytes 5308424 | tf_op jit(solution)/shard_map/ppermute | solution.py:18
  638.1 43.9 %collective-permute-start.2 = (f32[9,192,256]{2,1,0:T(8,128)S(1)}, f32[9,192,256]{2,1,0:T(8,128)}, u32[]{:S(2)}, u32[]{:S(2)}) collective-permute-start(f32[9,192,256]{2,1,0:T(8,128)S(1)} %copy.87), channel_id=1, source_target_pairs={{0,8},{8,16},{16,24},{24,32},{32,40},{40,48},{48,56},{56,64},{64,7... | collective-permute-start | bytes 5308424 | tf_op jit(solution)/shard_map/ppermute | solution.py:15
  946.6 12.0 %copy-start.4 = (f32[9,24,8,32]{1,2,0,3:T(8,128)S(1)}, f32[9,24,8,32]{1,2,0,3:T(8,128)}, u32[]{:S(2)}) copy-start(f32[9,24,8,32]{1,2,0,3:T(8,128)} %copy.104) | copy-start | bytes 663556
  950.1 9.6 copy-start.10
  953.3 11.1 all-to-all-start.1
  958.7 161.1 %all-reduce.2.cloned.1.call-start = ((), (), s32[]{:S(2)}) async-start(), calls=%async_computation.4 | async-start | bytes 524288 | tf_op jit(solution)/shard_map/psum | solution.py:113
  959.9 8.5 copy-start.9
  968.4 4.4 copy-start.11
  970.7 1.0 copy-start.5
  972.8 1.7 copy-start.8
  974.5 147.0 %copy-start.1 = (f32[9,192,192]{2,1,0:T(8,128)S(1)}, f32[9,192,192]{2,1,0:T(8,128)}, u32[]{:S(2)}) copy-start(f32[9,192,192]{2,1,0:T(8,128)} %param.12) | copy-start | bytes 3981316
  976.7 2.6 copy-start.6
Sparse Core Ops, SparseCore 0:
  9.8 30.0 all-gather.2
  605.5 24.9 all-gather.4
  977.6 142.1 all-reduce.1
where the time goes:
time: 1140 us; the launch traced here: 1130 us
  local copies, waits for them, and re-layouts  277 us (24%)
  waiting for transfers between devices  274 us (24%)
  blocking collectives  221 us (19%)
  matrix products  163 us (14%)
  loops' own time  106 us (9%)
  other arithmetic  56.2 us (5%)
  starting transfers between devices  16.5 us (1%)
  between operations  13.9 us (1%)
    gather x54, local copies, waits for them, and re-layouts, accumulate(): gathered = jnp.take(extended, local_ids[:, offset], axis=0)  171 us
    dot_general x54, matrix products, accumulate(): jnp.einsum('brc,bcm->brm', force_slice, gathered, precision=lax.Precision...  152 us
    psum x1, blocking collectives, local(): lax.psum(jnp.einsum('ra,rj->aj', flat_x, image_x, precision=lax.Precision...  141 us
    psum x1, waiting for transfers between devices, local(): lax.psum(local_gram(flat_x, full_w, vectors, w_block, image_x, hw_block,...  139 us
    another operation x2, loops' own time, apply_local(): lax.scan(accumulate, initial, jnp.arange(force_blocks.shape[1], dtype=jnp...  106 us
    psum x1, blocking collectives, local(): squares = lax.psum(jnp.sum(search_raw * search_raw, axis=(0, 1)), 'space')  69.6 us
    ppermute x2, waiting for transfers between devices, extended_2(): lax.ppermute(lax.slice_in_dim(block, 0, width, axis=dim), axis, backward)  69.4 us
    and x54, other arithmetic, accumulate(): gathered = jnp.take(extended, local_ids[:, offset], axis=0)  37.9 us
  transfers between devices with their start and end apart: 8, of which 8 were waited for; matrix products, arithmetic and copies ran while one was open for 2% of the time, Pallas kernels for 0%

commit v1 on v0

--- a/solution.py
+++ b/solution.py
@@ -4,6 +4,22 @@
 from jax.sharding import PartitionSpec as P
 
 CELLS = 9
+
+
+def collect(x, axis, dim):
+    ways, here, step = (lax.axis_size(axis), lax.axis_index(axis), x.shape[dim])
+    lengths = [n * ways if d == dim else n for d, n in enumerate(x.shape)]
+    full = lax.dynamic_update_slice_in_dim(jnp.zeros(lengths, x.dtype), x, here * step, axis=dim)
+    going_up = going_down = x
+    for far in range(1, ways // 2 + 1):
+        going_up = lax.ppermute(going_up, axis, [(d, (d + 1) % ways) for d in range(ways)])
+        full = lax.dynamic_update_slice_in_dim(full, going_up, (here - far) % ways * step, axis=dim)
+        if 2 * far < ways:
+            going_down = lax.ppermute(going_down, axis, [(d, (d - 1) % ways) for d in range(ways)])
+            full = lax.dynamic_update_slice_in_dim(
+                full, going_down, (here + far) % ways * step, axis=dim
+            )
+    return full
 
 
 def extended_2(block, sides, width):
@@ -45,7 +61,7 @@
 
 
 def spread_search(search_field):
-    gathered = lax.all_gather(search_field, "mode", axis=2, tiled=True)
+    gathered = collect(search_field, "mode", 2)
     extended = extended_2(gathered, (("space", 0),), CELLS)
     return (gathered, extended)
 

time: 1140 us -> 1170 us (1.026)
  local copies, waits for them, and re-layouts: 277 us -> 322 us
    dynamic_update_slice x0 -> x8, local copies, waits for them, and re-layouts: none -> 43.7 us  [the longest x4 21.8 us: collect(): lax.dynamic_update_slice_in_dim(full, going_up, (here - far) % ways * ste...]
    all_gather x1 -> x0, waiting for transfers between devices: 25.1 us -> none  [spread_search(): gathered = lax.all_gather(search_field, 'mode', axis=2, tiled=True)]
    ppermute x0 -> x7, local copies, waits for them, and re-layouts: none -> 15.3 us  [the longest x4 8.75 us: collect(): lax.ppermute(going_up, axis, [(d, (d + 1) % ways) for d in range(ways)])]
    ppermute x0 -> x7, waiting for transfers between devices: none -> 12.6 us  [the longest x4 12.4 us: collect(): lax.ppermute(going_up, axis, [(d, (d + 1) % ways) for d in range(ways)])]
    unnamed x32 -> x37, local copies, waits for them, and re-layouts: 32.5 us -> 24.6 us
  transfers between devices with their start and end apart: 8 -> 14, of which waited for: 8 -> 11; matrix products, arithmetic and copies ran while one was open for 2% -> 6% of each run, Pallas kernels for 0% -> 0%
where the time goes in v1:
time: 1170 us
  local copies, waits for them, and re-layouts  322 us (28%)
  waiting for transfers between devices  264 us (23%)
  blocking collectives  221 us (19%)
  matrix products  165 us (14%)
  loops' own time  106 us (9%)
  other arithmetic  55.1 us (5%)
  starting transfers between devices  20.5 us (2%)
  between operations  14.3 us (1%)
    gather x54, local copies, waits for them, and re-layouts, accumulate(): gathered = jnp.take(extended, local_ids[:, offset], axis=0)  171 us
    dot_general x54, matrix products, accumulate(): jnp.einsum('brc,bcm->brm', force_slice, gathered, precision=lax.Precision...  152 us
    psum x1, blocking collectives, local(): lax.psum(jnp.einsum('ra,rj->aj', flat_x, image_x, precision=lax.Precision...  141 us
    psum x1, waiting for transfers between devices, local(): lax.psum(local_gram(flat_x, full_w, vectors, w_block, image_x, hw_block,...  139 us
    another operation x2, loops' own time, apply_local(): lax.scan(accumulate, initial, jnp.arange(force_blocks.shape[1], dtype=jnp...  106 us
    ppermute x2, waiting for transfers between devices, extended_2(): lax.ppermute(lax.slice_in_dim(block, 0, width, axis=dim), axis, backward)  69.7 us
    psum x1, blocking collectives, local(): squares = lax.psum(jnp.sum(search_raw * search_raw, axis=(0, 1)), 'space')  69.6 us
    and x54, other arithmetic, accumulate(): gathered = jnp.take(extended, local_ids[:, offset], axis=0)  37.9 us
  transfers between devices with their start and end apart: 14, of which 11 were waited for; matrix products, arithmetic and copies ran while one was open for 6% of the time, Pallas kernels for 0%

profile of v1, /device:TPU:8, one launch (start us, length us, event | category | flops | bytes accessed | tf_op | source)
XLA Modules:
  0.0 1166.7 jit_solution(7379699624365530440)
XLA Ops:
  9.3 30.6 %all-gather.2.cloned.1.call-done = f32[9,192,256]{1,2,0:T(8,128)} async-done(((f32[9,192,32]{1,2,0:T(8,128)}), f32[9,192,256]{1,2,0:T(8,128)}) %all-gather.2.cloned.1.call-update) | async-done | bytes 1769488 | tf_op jit(solution)/shard_map/all_gather | solution.py:97
  42.0 5.5 collective-permute-start.1
  48.3 5.7 copy.97
  54.7 31.1 %collective-permute-done.1 = f32[9,192,256]{2,1,0:T(8,128)} collective-permute-done((f32[9,192,256]{2,1,0:T(8,128)S(1)}, f32[9,192,256]{2,1,0:T(8,128)}, u32[]{:S(2)}, u32[]{:S(2)}) %collective-permute-start.1) | collective-permute-done | bytes 1769504 | tf_op jit(solution)/shard_map/ppermute | solution.py:34
  94.3 5.2 pad_maximum_fusion
  99.5 7.6 copy.98
  107.2 248.9 %while.22 = (s32[]{:T(128)}, f32[9,24,256]{2,1,0:T(8,128)}, s32[27]{0:T(128)S(1)}, f32[9,27,24,192]{3,2,0,1:T(8,128)}, s32[9,27]{0,1:T(8,128)}, /*index=5*/f32[2...) while((s32[]{:T(128)}, f32[9,24,256]{2,1,0:T(8,128)}, s32[27]{0:T(128)S(1)}, ...), condition=%wide.region_1.3_spmd.clone, body=%wide.region_0.2_spmd.clone.sunk | while | flops 127956024 | bytes 5976391 | solution.py:56
  356.0 3.4 copy.99
  361.8 10.4 all_to_all.30
  375.9 3.4 copy.123
  384.1 141.0 %psum.21 = f32[256,32]{0,1:T(8,128)} all-reduce(f32[256,32]{0,1:T(8,128)} %fusion.27), channel_id=1, replica_groups=mesh['space'=32,'mode'=8] {'space'}, use_global_device_ids=true, to_apply=%region_2.4 | all-reduce | flops 8192 | bytes 65536 | tf_op jit(solution)/shard_map/psum | solution.py:102
  530.3 3.6 multiply_reduce_fusion
  533.8 69.6 %psum.22 = f32[32]{0:T(128)S(1)} all-reduce(f32[32]{0:T(128)S(1)} %get-tuple-element.203), channel_id=1, replica_groups=mesh['space'=32,'mode'=8] {'space'}, use_global_device_ids=true, to_apply=%region_4.6 | all-reduce | flops 32 | bytes 256 | tf_op jit(solution)/shard_map/psum | solution.py:123
  606.3 4.4 collective-permute-done.2
  612.7 4.1 collective-permute-done.4
  619.2 3.9 collective-permute-done.6
  624.5 6.1 dynamic_update_slice.24
  632.8 6.0 dynamic_update_slice.25
  641.0 6.0 dynamic_update_slice.26
  649.2 4.6 dynamic_update_slice.27
  656.0 4.2 dynamic_update_slice.28
  662.4 5.6 dynamic_update_slice.29
  670.2 5.6 dynamic_update_slice.30
  678.0 5.6 dynamic_update_slice.31
  686.1 38.6 %collective-permute-done.10 = f32[9,192,256]{2,1,0:T(8,128)} collective-permute-done((f32[9,192,256]{2,1,0:T(8,128)S(1)}, f32[9,192,256]{2,1,0:T(8,128)}, u32[]{:S(2)}, u32[]{:S(2)}) %collective-permute-start.10) | collective-permute-done | bytes 1769504 | tf_op jit(solution)/shard_map/ppermute | solution.py:34
  724.7 4.8 collective-permute-done.9
  729.4 4.9 pad_maximum_fusion.1
  734.4 248.9 %while.23 = (s32[]{:T(128)}, f32[9,24,256]{2,1,0:T(8,128)}, s32[27]{0:T(128)S(1)}, f32[9,27,24,192]{3,2,0,1:T(8,128)}, s32[9,27]{0,1:T(8,128)}, /*index=5*/f32[2...) while((s32[]{:T(128)}, f32[9,24,256]{2,1,0:T(8,128)}, s32[27]{0:T(128)S(1)}, ...), condition=%wide.region_6.8_spmd.clone, body=%wide.region_5.7_spmd.clone.sunk | while | flops 127956024 | bytes 5976391 | solution.py:56
  989.9 6.5 all-to-all-start.1
  997.8 4.3 all-to-all-done.1
  1011.6 3.8 fusion.22
  1019.1 139.1 %all-reduce.2.cloned.1.call-done = f32[512,4,32]{0,2,1:T(8,128)} async-done(((f32[512,4,32]{0,2,1:T(8,128)}), f32[512,4,32]{0,2,1:T(8,128)}) %all-reduce.2.cloned.1.call-update) | async-done | bytes 262160 | tf_op jit(solution)/shard_map/psum | solution.py:129
  (363 shorter events, 471.4 us)
Async XLA Ops:
  7.2 523.1 %copy-start = (f32[9,192,192]{2,1,0:T(8,128)S(1)}, f32[9,192,192]{2,1,0:T(8,128)}, u32[]{:S(2)}) copy-start(f32[9,192,192]{2,1,0:T(8,128)} %param.12) | copy-start | bytes 3981316
  7.2 32.8 %all-gather.2.cloned.1.call-start = ((), (), s32[]{:S(2)}) async-start(), calls=%async_computation.2 | async-start | bytes 2654208 | tf_op jit(solution)/shard_map/all_gather | solution.py:97
  42.0 12.0 %copy-start.2 = (f32[9,192,256]{2,1,0:T(8,128)}, f32[9,192,256]{2,1,0:T(8,128)S(1)}, u32[]{:S(2)}) copy-start(f32[9,192,256]{2,1,0:T(8,128)S(1)} %copy.93) | copy-start | bytes 5308420
  42.0 43.8 %collective-permute-start.1 = (f32[9,192,256]{2,1,0:T(8,128)S(1)}, f32[9,192,256]{2,1,0:T(8,128)}, u32[]{:S(2)}, u32[]{:S(2)}) collective-permute-start(f32[9,192,256]{2,1,0:T(8,128)S(1)} %copy.93), channel_id=1, source_target_pairs={{8,0},{16,8},{24,16},{32,24},{40,32},{48,40},{56,48},{64,56},{72,6... | collective-permute-start | bytes 5308424 | tf_op jit(solution)/shard_map/ppermute | solution.py:34
  47.5 43.9 %collective-permute-start = (f32[9,192,256]{2,1,0:T(8,128)S(1)}, f32[9,192,256]{2,1,0:T(8,128)}, u32[]{:S(2)}, u32[]{:S(2)}) collective-permute-start(f32[9,192,256]{2,1,0:T(8,128)S(1)} %copy.93), channel_id=1, source_target_pairs={{0,8},{8,16},{16,24},{24,32},{32,40},{40,48},{48,56},{56,64},{64,7... | collective-permute-start | bytes 5308424 | tf_op jit(solution)/shard_map/ppermute | solution.py:31
  375.9 5.7 copy-start.3
  604.5 18.6 %copy-start.9 = (f32[9,192,32]{1,2,0:T(8,128)}, f32[9,192,32]{1,2,0:T(8,128)S(1)}, u32[]{:S(2)}) copy-start(f32[9,192,32]{1,2,0:T(8,128)S(1)} %multiply_bitcast_fusion) | copy-start | bytes 663556
  604.5 6.2 collective-permute-start.2
  604.6 6.1 collective-permute-start.3
  610.7 12.4 %copy-start.14 = (f32[9,192,32]{1,2,0:T(8,128)}, f32[9,192,32]{1,2,0:T(8,128)S(1)}, u32[]{:S(2)}) copy-start(f32[9,192,32]{1,2,0:T(8,128)S(1)} %collective-permute-done.2) | copy-start | bytes 663556
  610.7 6.1 collective-permute-start.4
  610.7 12.4 %copy-start.12 = (f32[9,192,32]{1,2,0:T(8,128)}, f32[9,192,32]{1,2,0:T(8,128)S(1)}, u32[]{:S(2)}) copy-start(f32[9,192,32]{1,2,0:T(8,128)S(1)} %collective-permute-done.3) | copy-start | bytes 663556
  610.7 6.3 collective-permute-start.5
  616.8 6.3 copy-start.13
  616.8 6.3 collective-permute-start.6
  617.0 51.0 %collective-permute-start.7 = (f32[9,192,32]{1,2,0:T(8,128)}, f32[9,192,32]{1,2,0:T(8,128)}, u32[]{:S(2)}, u32[]{:S(2)}) collective-permute-start(f32[9,192,32]{1,2,0:T(8,128)} %collective-permute-done.5), channel_id=1, source_target_pairs={{0,7},{1,0},{2,1},{3,2},{4,3},{5,4},{6,5},{7,6},{8,15},{9,8},{10,9... | collective-permute-start | bytes 663560 | tf_op jit(solution)/shard_map/ppermute | solution.py:18
  623.1 52.7 %collective-permute-start.8 = (f32[9,192,32]{1,2,0:T(8,128)}, f32[9,192,32]{1,2,0:T(8,128)}, u32[]{:S(2)}, u32[]{:S(2)}) collective-permute-start(f32[9,192,32]{1,2,0:T(8,128)} %collective-permute-done.6), channel_id=1, source_target_pairs={{0,1},{1,2},{2,3},{3,4},{4,5},{5,6},{6,7},{7,0},{8,9},{9,10},{10,1... | collective-permute-start | bytes 663560 | tf_op jit(solution)/shard_map/ppermute | solution.py:15
  683.6 50.7 %copy-start.4 = (f32[9,192,256]{2,1,0:T(8,128)}, f32[9,192,256]{2,1,0:T(8,128)S(1)}, u32[]{:S(2)}) copy-start(f32[9,192,256]{2,1,0:T(8,128)S(1)} %dynamic_update_slice.31) | copy-start | bytes 5308420
  683.7 41.0 %collective-permute-start.10 = (f32[9,192,256]{2,1,0:T(8,128)S(1)}, f32[9,192,256]{2,1,0:T(8,128)}, u32[]{:S(2)}, u32[]{:S(2)}) collective-permute-start(f32[9,192,256]{2,1,0:T(8,128)S(1)} %dynamic_update_slice.31), channel_id=1, source_target_pairs={{8,0},{16,8},{24,16},{32,24},{40,32},{48,40},{56,48},{64,56},{72,6... | collective-permute-start | bytes 5308424 | tf_op jit(solution)/shard_map/ppermute | solution.py:34
  685.7 43.7 %collective-permute-start.9 = (f32[9,192,256]{2,1,0:T(8,128)S(1)}, f32[9,192,256]{2,1,0:T(8,128)}, u32[]{:S(2)}, u32[]{:S(2)}) collective-permute-start(f32[9,192,256]{2,1,0:T(8,128)S(1)} %dynamic_update_slice.31), channel_id=1, source_target_pairs={{0,8},{8,16},{16,24},{24,32},{32,40},{40,48},{48,56},{56,64},{64,7... | collective-permute-start | bytes 5308424 | tf_op jit(solution)/shard_map/ppermute | solution.py:31
  986.6 9.7 copy-start.5
  986.7 10.8 copy-start.10
  989.9 12.3 %all-to-all-start.1 = ((f32[8,1,6912]{2,1,0:T(1,128)}), f32[8,1,6912]{2,1,0:T(1,128)}, u32[]{:S(2)}, u32[]{:S(2)}) async-start(f32[8,1,6912]{2,1,0:T(1,128)} %reshape.72), calls=%async_computation.1 | async-start | bytes 442368 | tf_op jit(solution)/shard_map/all_to_all | solution.py:59
  996.4 161.8 %all-reduce.2.cloned.1.call-start = ((), (), s32[]{:S(2)}) async-start(), calls=%async_computation.3 | async-start | bytes 524288 | tf_op jit(solution)/shard_map/psum | solution.py:129
  997.6 8.5 copy-start.8
  1006.1 4.4 copy-start.11
  1008.4 1.0 copy-start.6
  1011.6 148.2 %copy-start.1 = (f32[9,192,192]{2,1,0:T(8,128)S(1)}, f32[9,192,192]{2,1,0:T(8,128)}, u32[]{:S(2)}) copy-start(f32[9,192,192]{2,1,0:T(8,128)} %param.12) | copy-start | bytes 3981316
  1015.4 2.6 copy-start.7
Sparse Core Ops, SparseCore 0:
  9.8 30.0 all-gather.1
  1016.3 141.8 all-reduce.1
